TPU v7x, 512 devices: a whole 4x8x8 slice. The times are simulated.
512 devices in a mesh: sec: 4 (over x), lat: 8 (over z), lon: 16 (over y, core).
Axes of the slice: x: 4, y: 8, z: 8, core: 2. Of those that a mesh axis runs over, the one named last changes fastest.
Arguments:
- state: float32 [4, 75, 32, 2048], P('sec', None, 'lat', 'lon'), may hold values from -6 to 6
- mixing: bfloat16 [4, 75, 32, 2048], P('sec', None, 'lat', 'lon'), may hold values from 0.05 to 50
- eastward: bfloat16 [4, 75, 32, 2048], P('sec', None, 'lat', 'lon'), may hold values from -0.44921875 to 0.44921875
- northward: bfloat16 [4, 75, 32, 2048], P('sec', None, 'lat', 'lon'), may hold values from -0.44921875 to 0.44921875
- sea_mask: int32 [32, 2048], P('lat', 'lon'), may hold values 0 or 1
- weights: bfloat16 [4, 8, 16, 16, 16, 512], P('sec', 'lat', 'lon'), may hold values from -1.5 to 1.5
- source_block: int32 [4, 8, 16, 128, 4], P('sec', 'lat', 'lon'), may hold values from 0 to 31
- dest_block: int32 [4, 8, 16, 128, 4], P('sec', 'lat', 'lon'), may hold values from 0 to 31
- record_counts: int32 [4, 8, 16, 128], P('sec', 'lat', 'lon'), may hold values from 0 to 4, as said below
Outputs:
- adjoint: float32 [4, 75, 32, 2048], P('sec', None, 'lat', 'lon')
Inputs may be any that keep to these rules, and one draw needn't show every extreme that they name: `record_counts`: in every section some receiving device has 4 live slots from every sending device.
All inputs are finite; a program needn't handle non-finite values. No bound on the sum of `sea_mask` on one device may be relied on, other than what follows from the above.
Results may differ from a plain program's by a relative error of at most 0.0003.
Values sent between devices are 32-bit elements; how exact they have to be, the bound alone decides.
No kernel may reach another device: no remote copies, remote signals or barrier semaphores. Data moves between devices by JAX's collectives and lax.ppermute only.
A program may use at most 64 MiB of HBM per device.

v0:
```python
import jax
import jax.numpy as jnp
from jax import lax
from jax.sharding import PartitionSpec as P

NCPL = 4
NSUB = 2


def extended(block, sides, width, periodic):
    for axis, dim in sides:
        count = lax.axis_size(axis)
        forward = [(i, i + 1) for i in range(count - 1)]
        if periodic:
            forward.append((count - 1, 0))
        backward = [(target, source) for source, target in forward]
        low = lax.ppermute(
            lax.slice_in_dim(block, block.shape[dim] - width, None, axis=dim), axis, forward
        )
        high = lax.ppermute(lax.slice_in_dim(block, 0, width, axis=dim), axis, backward)
        block = jnp.concatenate([low, block, high], axis=dim)
    return block


def column_solve(right, coeff):
    zero_row = jnp.zeros_like(coeff[:1])
    lower_band = jnp.concatenate([zero_row, coeff[1:]], axis=0)
    upper_band = jnp.concatenate([coeff[1:], zero_row], axis=0)
    centre = 1.0 + lower_band + upper_band

    def sweep_down(carried, entries):
        prior_c, prior_z = carried
        centre_k, beneath, overhead, right_k = entries
        pivot_value = centre_k + beneath * prior_c
        factor = -overhead / pivot_value
        partial_value = (right_k + beneath * prior_z) / pivot_value
        return ((factor, partial_value), (factor, partial_value))

    start_pair = (jnp.zeros_like(right[0]), jnp.zeros_like(right[0]))
    _, (factors, partials) = lax.scan(
        sweep_down, start_pair, (centre, lower_band, upper_band, right)
    )

    def sweep_up(carried, entries):
        factor, partial_value = entries
        solved_k = partial_value - factor * carried
        return (solved_k, solved_k)

    _, solved = lax.scan(sweep_up, jnp.zeros_like(right[0]), (factors, partials), reverse=True)
    return solved


def advect(mixed_adj, east_speed, north_speed):
    east_flux = east_speed.astype(jnp.float32) * mixed_adj
    north_flux = north_speed.astype(jnp.float32) * mixed_adj
    east_rim = extended(east_flux, (("lon", 2),), 1, True)
    north_rim = extended(north_flux, (("lat", 1),), 1, False)
    east_diff = east_rim[:, :, 2:] - east_rim[:, :, :-2]
    north_diff = north_rim[:, 2:, :] - north_rim[:, :-2, :]
    return mixed_adj + 0.5 * (east_diff + north_diff)


def couple(field_part, weights, source_block, dest_block, record_counts, air_factor):
    block_cells = weights.shape[3]
    capacity = source_block.shape[-1]
    peer_count = record_counts.shape[-1]
    surface = field_part[-1].reshape(-1, block_cells)
    block_count = surface.shape[0]
    gathered = jnp.take(surface, source_block.reshape(-1), axis=0)
    weight_table = weights[0, 0, 0].astype(jnp.float32)
    contribution = jnp.einsum("diz,zi->dz", weight_table, gathered, precision=lax.Precision.HIGHEST)
    received = lax.all_to_all(
        contribution.reshape(block_cells, peer_count, capacity),
        ("lat", "lon"),
        split_axis=1,
        concat_axis=1,
        tiled=True,
    )
    arrived = received.reshape(block_cells, peer_count * capacity)
    live_slot = (
        jnp.arange(capacity, dtype=jnp.int32)[None, :] < record_counts[0, 0, 0][:, None]
    ).reshape(-1)
    matches = dest_block.reshape(-1)[:, None] == jnp.arange(block_count, dtype=jnp.int32)[None, :]
    one_hot = jnp.logical_and(matches, live_slot[:, None]).astype(jnp.float32)
    accumulated = jnp.dot(
        arrived, one_hot, precision=lax.Precision.HIGHEST, preferred_element_type=jnp.float32
    )
    summed = lax.psum(accumulated * air_factor, "sec")
    return summed.T.reshape(field_part.shape[1], field_part.shape[2])


def local(
    state, mixing, eastward, northward, sea_mask, weights, source_block, dest_block, record_counts
):
    section = lax.axis_index("sec")
    section_count = lax.axis_size("sec")
    is_ocean = section == section_count - 1
    air_factor = jnp.where(is_ocean, 0.0, 1.0).astype(jnp.float32)
    ocean_keep = sea_mask.astype(jnp.float32)
    keep_factor = jnp.where(is_ocean, ocean_keep, jnp.ones_like(ocean_keep))
    field_part = state[0]
    mix_part = mixing[0]
    east_part = eastward[0]
    north_part = northward[0]
    for coupling in range(NCPL):
        for repeat in range(NSUB):
            mixed_adj = column_solve(field_part, mix_part.astype(jnp.float32))
            field_part = advect(mixed_adj, east_part, north_part) * keep_factor
        forcing = couple(field_part, weights, source_block, dest_block, record_counts, air_factor)
        field_part = field_part.at[0].add(
            jnp.where(is_ocean, forcing * ocean_keep, jnp.zeros_like(forcing))
        )
    return field_part[None]


def solution(mesh):
    in_specs = (
        P("sec", None, "lat", "lon"),
        P("sec", None, "lat", "lon"),
        P("sec", None, "lat", "lon"),
        P("sec", None, "lat", "lon"),
        P("lat", "lon"),
        P("sec", "lat", "lon", None, None, None),
        P("sec", "lat", "lon", None, None),
        P("sec", "lat", "lon", None, None),
        P("sec", "lat", "lon", None),
    )
    out_specs = P("sec", None, "lat", "lon")
    return jax.shard_map(local, mesh=mesh, in_specs=in_specs, out_specs=out_specs, check_vma=False)
```

profile of v0, /device:TPU:2, one launch (start us, length us, event | category | flops | bytes accessed | tf_op | source)
XLA Modules:
  0.0 362.5 jit_solution(979839688588339115)
XLA Ops:
  1.1 52.6 %while.276 = (s32[]{:T(128)}, f32[4,128]{1,0:T(4,128)S(1)}, f32[4,128]{1,0:T(4,128)S(1)}, f32[75,4,128]{2,1,0:T(4,128)S(1)}, f32[75,4,128]{2,1,0:T(4,128)S(1)}, ...) while((s32[]{:T(128)}, f32[4,128]{1,0:T(4,128)S(1)}, ...), condition=%wide.region_1.2_spmd.clone, body=%wide.region_0.1_spmd.clone.sunk | while | flops 4611 | bytes 20603 | solution.py:40
  53.7 2.7 while.277
  57.6 2.9 collective-permute-start
  61.9 4.9 %collective-permute-start.3 = (f32[75,1,128]{2,1,0:T(1,128)S(1)}, f32[75,1,128]{2,1,0:T(1,128)S(1)}, u32[]{:S(2)}, u32[]{:S(2)}) collective-permute-start(f32[75,1,128]{2,1,0:T(1,128)S(1)} %get-tuple-element.2005), channel_id=1, source_target_pairs={{0,16},{16,32},{32,48},{48,64},{64,80},{80,96},{96,112},{1,17},{17... | collective-permute-start | bytes 115208 | tf_op jit(solution)/shard_map/ppermute | solution.py:17
  68.9 3.2 while.278
  72.1 2.7 while.279
  79.8 4.9 %collective-permute-start.7 = (f32[75,1,128]{2,1,0:T(1,128)}, f32[75,1,128]{2,1,0:T(1,128)S(1)}, u32[]{:S(2)}, u32[]{:S(2)}) collective-permute-start(f32[75,1,128]{2,1,0:T(1,128)} %get-tuple-element.1999), channel_id=1, source_target_pairs={{0,16},{16,32},{32,48},{48,64},{64,80},{80,96},{96,112},{1,17},{17... | collective-permute-start | bytes 115208 | tf_op jit(solution)/shard_map/ppermute | solution.py:17
  89.5 2.6 fusion.127
  92.1 16.9 %all-to-all-start = ((f32[16,128,4]{0,2,1:T(4,128)}), f32[16,128,4]{0,2,1:T(4,128)S(1)}, u32[]{:S(2)}, u32[]{:S(2)}) async-start(f32[16,128,4]{0,2,1:T(4,128)} %bitcast.13), calls=%async_computation | async-start | bytes 524288 | tf_op jit(solution)/shard_map/all_to_all | solution.py:72
  109.5 14.2 %all-to-all-done = f32[16,128,4]{0,2,1:T(4,128)S(1)} async-done(((f32[16,128,4]{0,2,1:T(4,128)}), f32[16,128,4]{0,2,1:T(4,128)S(1)}, u32[]{:S(2)}, u32[]{:S(2)}) %all-to-all-start) | async-done | bytes 32800 | tf_op jit(solution)/shard_map/all_to_all | solution.py:72
  124.4 8.6 %psum.28 = f32[4,128]{1,0:T(4,128)S(1)} all-reduce(f32[4,128]{1,0:T(4,128)S(1)} %reshape.204), channel_id=1, replica_groups=mesh['sec'=4,'lat'=8,'lon'=16] {'sec'}, use_global_device_ids=true, to_apply=%region_8.10 | all-reduce | flops 512 | bytes 4096 | tf_op jit(solution)/shard_map/psum | solution.py:88
  133.1 3.2 while.280
  136.4 2.7 while.281
  141.1 5.2 %collective-permute-start.11 = (f32[75,1,128]{2,1,0:T(1,128)}, f32[75,1,128]{2,1,0:T(1,128)}, u32[]{:S(2)}, u32[]{:S(2)}) collective-permute-start(f32[75,1,128]{2,1,0:T(1,128)} %get-tuple-element.1993), channel_id=1, source_target_pairs={{0,16},{16,32},{32,48},{48,64},{64,80},{80,96},{96,112},{1,17},{17... | collective-permute-start | bytes 115208 | tf_op jit(solution)/shard_map/ppermute | solution.py:17
  147.6 2.5 collective-permute-done.8
  150.2 3.0 collective-permute-done.9
  155.2 3.0 while.282
  158.3 2.7 while.283
  162.5 4.7 %collective-permute-start.15 = (f32[75,1,128]{2,1,0:T(1,128)S(1)}, f32[75,1,128]{2,1,0:T(1,128)S(1)}, u32[]{:S(2)}, u32[]{:S(2)}) collective-permute-start(f32[75,1,128]{2,1,0:T(1,128)S(1)} %get-tuple-element.1987), channel_id=1, source_target_pairs={{0,16},{16,32},{32,48},{48,64},{64,80},{80,96},{96,112},{1,17},{17... | collective-permute-start | bytes 115208 | tf_op jit(solution)/shard_map/ppermute | solution.py:17
  170.1 3.1 collective-permute-done.13
  174.9 2.6 fusion.128
  177.5 7.4 %all-to-all-start.1 = ((f32[16,128,4]{0,2,1:T(4,128)}), f32[16,128,4]{0,2,1:T(4,128)S(1)}, u32[]{:S(2)}, u32[]{:S(2)}) async-start(f32[16,128,4]{0,2,1:T(4,128)} %bitcast.23), calls=%async_computation.1 | async-start | bytes 524288 | tf_op jit(solution)/shard_map/all_to_all | solution.py:72
  184.9 14.7 %all-to-all-done.1 = f32[16,128,4]{0,2,1:T(4,128)S(1)} async-done(((f32[16,128,4]{0,2,1:T(4,128)}), f32[16,128,4]{0,2,1:T(4,128)S(1)}, u32[]{:S(2)}, u32[]{:S(2)}) %all-to-all-start.1) | async-done | bytes 32800 | tf_op jit(solution)/shard_map/all_to_all | solution.py:72
  200.3 10.1 %psum.29 = f32[4,128]{1,0:T(4,128)S(1)} all-reduce(f32[4,128]{1,0:T(4,128)S(1)} %reshape.208), channel_id=1, replica_groups=mesh['sec'=4,'lat'=8,'lon'=16] {'sec'}, use_global_device_ids=true, to_apply=%region_17.19 | all-reduce | flops 512 | bytes 4096 | tf_op jit(solution)/shard_map/psum | solution.py:88
  210.5 3.2 while.284
  213.7 2.7 while.285
  218.5 5.2 %collective-permute-start.19 = (f32[75,1,128]{2,1,0:T(1,128)}, f32[75,1,128]{2,1,0:T(1,128)}, u32[]{:S(2)}, u32[]{:S(2)}) collective-permute-start(f32[75,1,128]{2,1,0:T(1,128)} %get-tuple-element.1981), channel_id=1, source_target_pairs={{0,16},{16,32},{32,48},{48,64},{64,80},{80,96},{96,112},{1,17},{17... | collective-permute-start | bytes 115208 | tf_op jit(solution)/shard_map/ppermute | solution.py:17
  227.5 3.0 collective-permute-done.17
  232.5 3.0 while.286
  235.6 2.7 while.287
  239.8 4.5 %collective-permute-start.23 = (f32[75,1,128]{2,1,0:T(1,128)S(1)}, f32[75,1,128]{2,1,0:T(1,128)S(1)}, u32[]{:S(2)}, u32[]{:S(2)}) collective-permute-start(f32[75,1,128]{2,1,0:T(1,128)S(1)} %get-tuple-element.1975), channel_id=1, source_target_pairs={{0,16},{16,32},{32,48},{48,64},{64,80},{80,96},{96,112},{1,17},{17... | collective-permute-start | bytes 115208 | tf_op jit(solution)/shard_map/ppermute | solution.py:17
  247.2 3.1 collective-permute-done.21
  252.0 2.6 fusion.129
  254.6 7.4 %all-to-all-start.2 = ((f32[16,128,4]{0,2,1:T(4,128)}), f32[16,128,4]{0,2,1:T(4,128)S(1)}, u32[]{:S(2)}, u32[]{:S(2)}) async-start(f32[16,128,4]{0,2,1:T(4,128)} %bitcast.32), calls=%async_computation.2 | async-start | bytes 524288 | tf_op jit(solution)/shard_map/all_to_all | solution.py:72
  262.0 14.7 %all-to-all-done.2 = f32[16,128,4]{0,2,1:T(4,128)S(1)} async-done(((f32[16,128,4]{0,2,1:T(4,128)}), f32[16,128,4]{0,2,1:T(4,128)S(1)}, u32[]{:S(2)}, u32[]{:S(2)}) %all-to-all-start.2) | async-done | bytes 32800 | tf_op jit(solution)/shard_map/all_to_all | solution.py:72
  277.4 7.7 %psum.30 = f32[4,128]{1,0:T(4,128)S(1)} all-reduce(f32[4,128]{1,0:T(4,128)S(1)} %reshape.212), channel_id=1, replica_groups=mesh['sec'=4,'lat'=8,'lon'=16] {'sec'}, use_global_device_ids=true, to_apply=%region_26.28 | all-reduce | flops 512 | bytes 4096 | tf_op jit(solution)/shard_map/psum | solution.py:88
  285.2 3.2 while.288
  288.4 2.7 while.289
  293.2 5.2 %collective-permute-start.27 = (f32[75,1,128]{2,1,0:T(1,128)}, f32[75,1,128]{2,1,0:T(1,128)}, u32[]{:S(2)}, u32[]{:S(2)}) collective-permute-start(f32[75,1,128]{2,1,0:T(1,128)} %get-tuple-element.1969), channel_id=1, source_target_pairs={{0,16},{16,32},{32,48},{48,64},{64,80},{80,96},{96,112},{1,17},{17... | collective-permute-start | bytes 115208 | tf_op jit(solution)/shard_map/ppermute | solution.py:17
  302.3 3.0 collective-permute-done.25
  307.3 3.0 while.290
  310.4 2.7 while.291
  314.5 4.5 %collective-permute-start.31 = (f32[75,1,128]{2,1,0:T(1,128)S(1)}, f32[75,1,128]{2,1,0:T(1,128)S(1)}, u32[]{:S(2)}, u32[]{:S(2)}) collective-permute-start(f32[75,1,128]{2,1,0:T(1,128)S(1)} %get-tuple-element.1963), channel_id=1, source_target_pairs={{0,16},{16,32},{32,48},{48,64},{64,80},{80,96},{96,112},{1,17},{17... | collective-permute-start | bytes 115208 | tf_op jit(solution)/shard_map/ppermute | solution.py:17
  322.0 3.1 collective-permute-done.29
  326.8 2.6 fusion.130
  329.4 7.4 %all-to-all-start.3 = ((f32[16,128,4]{0,2,1:T(4,128)}), f32[16,128,4]{0,2,1:T(4,128)S(1)}, u32[]{:S(2)}, u32[]{:S(2)}) async-start(f32[16,128,4]{0,2,1:T(4,128)} %bitcast.42), calls=%async_computation.3 | async-start | bytes 524288 | tf_op jit(solution)/shard_map/all_to_all | solution.py:72
  337.4 14.0 %all-to-all-done.3 = f32[16,128,4]{0,2,1:T(4,128)S(1)} async-done(((f32[16,128,4]{0,2,1:T(4,128)}), f32[16,128,4]{0,2,1:T(4,128)S(1)}, u32[]{:S(2)}, u32[]{:S(2)}) %all-to-all-start.3) | async-done | bytes 32800 | tf_op jit(solution)/shard_map/all_to_all | solution.py:72
  352.1 9.7 %psum.31 = f32[4,128]{1,0:T(4,128)S(1)} all-reduce(f32[4,128]{1,0:T(4,128)S(1)} %reshape.216), channel_id=1, replica_groups=mesh['sec'=4,'lat'=8,'lon'=16] {'sec'}, use_global_device_ids=true, to_apply=%region_35.37 | all-reduce | flops 512 | bytes 4096 | tf_op jit(solution)/shard_map/psum | solution.py:88
  (1398 shorter events, 133.6 us)
Async XLA Ops:
  0.0 66.8 %copy-start.9 = (s32[1,1,1,128,4]{3,4,2,1,0:T(4,128)S(1)}, s32[1,1,1,128,4]{3,4,2,1,0:T(4,128)}, u32[]{:S(2)}) copy-start(s32[1,1,1,128,4]{3,4,2,1,0:T(4,128)} %param.57) | copy-start | bytes 6148
  0.0 67.1 %copy-start.6 = (s32[4,128]{1,0:T(4,128)S(1)}, s32[4,128]{1,0:T(4,128)}, u32[]{:S(2)}) copy-start(s32[4,128]{1,0:T(4,128)} %param.55) | copy-start | bytes 6148
  1.1 73.8 %copy-start = (bf16[1,75,4,128]{3,2,1,0:T(4,128)(2,1)S(1)}, bf16[1,75,4,128]{3,2,1,0:T(4,128)(2,1)}, u32[]{:S(2)}) copy-start(bf16[1,75,4,128]{3,2,1,0:T(4,128)(2,1)} %param.53) | copy-start | bytes 230404
  1.1 73.8 %copy-start.1 = (bf16[1,75,4,128]{3,2,1,0:T(4,128)(2,1)S(1)}, bf16[1,75,4,128]{3,2,1,0:T(4,128)(2,1)}, u32[]{:S(2)}) copy-start(bf16[1,75,4,128]{3,2,1,0:T(4,128)(2,1)} %param.54) | copy-start | bytes 230404
  57.4 27.3 %copy-start.2 = (bf16[1,1,1,16,16,512]{5,4,3,2,1,0:T(8,128)(2,1)S(1)}, bf16[1,1,1,16,16,512]{5,4,3,2,1,0:T(8,128)(2,1)}, u32[]{:S(2)}) copy-start(bf16[1,1,1,16,16,512]{5,4,3,2,1,0:T(8,128)(2,1)} %param.56) | copy-start | bytes 786436
  57.6 9.5 %collective-permute-start = (f32[75,4,1]{2,1,0:T(4,128)S(1)}, f32[75,4,1]{2,1,0:T(4,128)S(1)}, u32[]{:S(2)}, u32[]{:S(2)}) collective-permute-start(f32[75,4,1]{2,1,0:T(4,128)S(1)} %get-tuple-element.2000), channel_id=1, source_target_pairs={{1,0},{2,1},{3,2},{4,3},{5,4},{6,5},{7,6},{8,7},{9,8},{10,9},{11,1... | collective-permute-start | bytes 3608 | tf_op jit(solution)/shard_map/ppermute | solution.py:20
  60.5 6.6 %collective-permute-start.1 = (f32[75,4,1]{2,1,0:T(4,128)S(1)}, f32[75,4,1]{2,1,0:T(4,128)S(1)}, u32[]{:S(2)}, u32[]{:S(2)}) collective-permute-start(f32[75,4,1]{2,1,0:T(4,128)S(1)} %get-tuple-element.2001), channel_id=1, source_target_pairs={{0,1},{1,2},{2,3},{3,4},{4,5},{5,6},{6,7},{7,8},{8,9},{9,10},{10,1... | collective-permute-start | bytes 3608 | tf_op jit(solution)/shard_map/ppermute | solution.py:17
  60.6 6.6 %collective-permute-start.2 = (f32[75,1,128]{2,1,0:T(1,128)S(1)}, f32[75,1,128]{2,1,0:T(1,128)S(1)}, u32[]{:S(2)}, u32[]{:S(2)}) collective-permute-start(f32[75,1,128]{2,1,0:T(1,128)S(1)} %get-tuple-element.2004), channel_id=1, source_target_pairs={{16,0},{32,16},{48,32},{64,48},{80,64},{96,80},{112,96},{17,1},{33... | collective-permute-start | bytes 115208 | tf_op jit(solution)/shard_map/ppermute | solution.py:20
  61.9 6.5 %collective-permute-start.3 = (f32[75,1,128]{2,1,0:T(1,128)S(1)}, f32[75,1,128]{2,1,0:T(1,128)S(1)}, u32[]{:S(2)}, u32[]{:S(2)}) collective-permute-start(f32[75,1,128]{2,1,0:T(1,128)S(1)} %get-tuple-element.2005), channel_id=1, source_target_pairs={{0,16},{16,32},{32,48},{48,64},{64,80},{80,96},{96,112},{1,17},{17... | collective-permute-start | bytes 115208 | tf_op jit(solution)/shard_map/ppermute | solution.py:17
  67.1 22.3 %copy-start.7 = (pred[512]{0:T(512)(128)(4,1)}, pred[512]{0:T(512)(128)(4,1)S(1)}, u32[]{:S(2)}) copy-start(pred[512]{0:T(512)(128)(4,1)S(1)} %compare_and_fusion) | copy-start | bytes 1540
  75.8 11.1 %collective-permute-start.4 = (f32[75,4,1]{2,1,0:T(4,128)}, f32[75,4,1]{2,1,0:T(4,128)}, u32[]{:S(2)}, u32[]{:S(2)}) collective-permute-start(f32[75,4,1]{2,1,0:T(4,128)} %get-tuple-element.1994), channel_id=1, source_target_pairs={{1,0},{2,1},{3,2},{4,3},{5,4},{6,5},{7,6},{8,7},{9,8},{10,9},{11,1... | collective-permute-start | bytes 3608 | tf_op jit(solution)/shard_map/ppermute | solution.py:20
  77.9 9.0 %collective-permute-start.5 = (f32[75,4,1]{2,1,0:T(4,128)}, f32[75,4,1]{2,1,0:T(4,128)}, u32[]{:S(2)}, u32[]{:S(2)}) collective-permute-start(f32[75,4,1]{2,1,0:T(4,128)} %get-tuple-element.1995), channel_id=1, source_target_pairs={{0,1},{1,2},{2,3},{3,4},{4,5},{5,6},{6,7},{7,8},{8,9},{9,10},{10,1... | collective-permute-start | bytes 3608 | tf_op jit(solution)/shard_map/ppermute | solution.py:17
  78.6 8.3 %collective-permute-start.6 = (f32[75,1,128]{2,1,0:T(1,128)}, f32[75,1,128]{2,1,0:T(1,128)S(1)}, u32[]{:S(2)}, u32[]{:S(2)}) collective-permute-start(f32[75,1,128]{2,1,0:T(1,128)} %get-tuple-element.1998), channel_id=1, source_target_pairs={{16,0},{32,16},{48,32},{64,48},{80,64},{96,80},{112,96},{17,1},{33... | collective-permute-start | bytes 115208 | tf_op jit(solution)/shard_map/ppermute | solution.py:20
  79.8 7.0 %collective-permute-start.7 = (f32[75,1,128]{2,1,0:T(1,128)}, f32[75,1,128]{2,1,0:T(1,128)S(1)}, u32[]{:S(2)}, u32[]{:S(2)}) collective-permute-start(f32[75,1,128]{2,1,0:T(1,128)} %get-tuple-element.1999), channel_id=1, source_target_pairs={{0,16},{16,32},{32,48},{48,64},{64,80},{80,96},{96,112},{1,17},{17... | collective-permute-start | bytes 115208 | tf_op jit(solution)/shard_map/ppermute | solution.py:17
  89.4 19.7 %copy-start.11 = (s32[1,1,1,128]{3,2,1,0:T(1,128)S(1)}, s32[1,1,1,128]{3,2,1,0:T(1,128)}, u32[]{:S(2)}) copy-start(s32[1,1,1,128]{3,2,1,0:T(1,128)} %param.59) | copy-start | bytes 1540
  89.4 19.8 %copy-start.10 = (s32[1,1,1,128,4]{3,4,2,1,0:T(4,128)S(1)}, s32[1,1,1,128,4]{3,4,2,1,0:T(4,128)}, u32[]{:S(2)}) copy-start(s32[1,1,1,128,4]{3,4,2,1,0:T(4,128)} %param.58) | copy-start | bytes 6148
  92.1 31.6 %all-to-all-start = ((f32[16,128,4]{0,2,1:T(4,128)}), f32[16,128,4]{0,2,1:T(4,128)S(1)}, u32[]{:S(2)}, u32[]{:S(2)}) async-start(f32[16,128,4]{0,2,1:T(4,128)} %bitcast.13), calls=%async_computation | async-start | bytes 524288 | tf_op jit(solution)/shard_map/all_to_all | solution.py:72
  139.9 13.3 %collective-permute-start.10 = (f32[75,1,128]{2,1,0:T(1,128)}, f32[75,1,128]{2,1,0:T(1,128)}, u32[]{:S(2)}, u32[]{:S(2)}) collective-permute-start(f32[75,1,128]{2,1,0:T(1,128)} %get-tuple-element.1992), channel_id=1, source_target_pairs={{16,0},{32,16},{48,32},{64,48},{80,64},{96,80},{112,96},{17,1},{33... | collective-permute-start | bytes 115208 | tf_op jit(solution)/shard_map/ppermute | solution.py:20
  141.1 12.7 %collective-permute-start.11 = (f32[75,1,128]{2,1,0:T(1,128)}, f32[75,1,128]{2,1,0:T(1,128)}, u32[]{:S(2)}, u32[]{:S(2)}) collective-permute-start(f32[75,1,128]{2,1,0:T(1,128)} %get-tuple-element.1993), channel_id=1, source_target_pairs={{0,16},{16,32},{32,48},{48,64},{64,80},{80,96},{96,112},{1,17},{17... | collective-permute-start | bytes 115208 | tf_op jit(solution)/shard_map/ppermute | solution.py:17
  147.1 3.1 collective-permute-start.8
  147.1 6.1 %collective-permute-start.9 = (f32[75,4,1]{2,1,0:T(4,128)}, f32[75,4,1]{2,1,0:T(4,128)S(1)}, u32[]{:S(2)}, u32[]{:S(2)}) collective-permute-start(f32[75,4,1]{2,1,0:T(4,128)} %get-tuple-element.1989), channel_id=1, source_target_pairs={{0,1},{1,2},{2,3},{3,4},{4,5},{5,6},{6,7},{7,8},{8,9},{9,10},{10,1... | collective-permute-start | bytes 3608 | tf_op jit(solution)/shard_map/ppermute | solution.py:17
  153.2 0.7 copy-start.3
  161.1 13.7 %copy-start.8 = (pred[512]{0:T(512)(128)(4,1)S(1)}, pred[512]{0:T(512)(128)(4,1)}, u32[]{:S(2)}) copy-start(pred[512]{0:T(512)(128)(4,1)} %copy-done.7) | copy-start | bytes 1540
  161.2 12.1 %collective-permute-start.14 = (f32[75,1,128]{2,1,0:T(1,128)S(1)}, f32[75,1,128]{2,1,0:T(1,128)S(1)}, u32[]{:S(2)}, u32[]{:S(2)}) collective-permute-start(f32[75,1,128]{2,1,0:T(1,128)S(1)} %get-tuple-element.1986), channel_id=1, source_target_pairs={{16,0},{32,16},{48,32},{64,48},{80,64},{96,80},{112,96},{17,1},{33... | collective-permute-start | bytes 115208 | tf_op jit(solution)/shard_map/ppermute | solution.py:20
  162.5 10.8 %collective-permute-start.15 = (f32[75,1,128]{2,1,0:T(1,128)S(1)}, f32[75,1,128]{2,1,0:T(1,128)S(1)}, u32[]{:S(2)}, u32[]{:S(2)}) collective-permute-start(f32[75,1,128]{2,1,0:T(1,128)S(1)} %get-tuple-element.1987), channel_id=1, source_target_pairs={{0,16},{16,32},{32,48},{48,64},{64,80},{80,96},{96,112},{1,17},{17... | collective-permute-start | bytes 115208 | tf_op jit(solution)/shard_map/ppermute | solution.py:17
  167.3 2.8 collective-permute-start.12
  167.4 5.9 %collective-permute-start.13 = (f32[75,4,1]{2,1,0:T(4,128)S(1)}, f32[75,4,1]{2,1,0:T(4,128)S(1)}, u32[]{:S(2)}, u32[]{:S(2)}) collective-permute-start(f32[75,4,1]{2,1,0:T(4,128)S(1)} %get-tuple-element.1983), channel_id=1, source_target_pairs={{0,1},{1,2},{2,3},{3,4},{4,5},{5,6},{6,7},{7,8},{8,9},{9,10},{10,1... | collective-permute-start | bytes 3608 | tf_op jit(solution)/shard_map/ppermute | solution.py:17
  177.5 22.1 %all-to-all-start.1 = ((f32[16,128,4]{0,2,1:T(4,128)}), f32[16,128,4]{0,2,1:T(4,128)S(1)}, u32[]{:S(2)}, u32[]{:S(2)}) async-start(f32[16,128,4]{0,2,1:T(4,128)} %bitcast.23), calls=%async_computation.1 | async-start | bytes 524288 | tf_op jit(solution)/shard_map/all_to_all | solution.py:72
  217.2 13.3 %collective-permute-start.18 = (f32[75,1,128]{2,1,0:T(1,128)}, f32[75,1,128]{2,1,0:T(1,128)}, u32[]{:S(2)}, u32[]{:S(2)}) collective-permute-start(f32[75,1,128]{2,1,0:T(1,128)} %get-tuple-element.1980), channel_id=1, source_target_pairs={{16,0},{32,16},{48,32},{64,48},{80,64},{96,80},{112,96},{17,1},{33... | collective-permute-start | bytes 115208 | tf_op jit(solution)/shard_map/ppermute | solution.py:20
  218.5 12.7 %collective-permute-start.19 = (f32[75,1,128]{2,1,0:T(1,128)}, f32[75,1,128]{2,1,0:T(1,128)}, u32[]{:S(2)}, u32[]{:S(2)}) collective-permute-start(f32[75,1,128]{2,1,0:T(1,128)} %get-tuple-element.1981), channel_id=1, source_target_pairs={{0,16},{16,32},{32,48},{48,64},{64,80},{80,96},{96,112},{1,17},{17... | collective-permute-start | bytes 115208 | tf_op jit(solution)/shard_map/ppermute | solution.py:17
  224.5 3.1 collective-permute-start.16
  224.5 6.1 %collective-permute-start.17 = (f32[75,4,1]{2,1,0:T(4,128)}, f32[75,4,1]{2,1,0:T(4,128)S(1)}, u32[]{:S(2)}, u32[]{:S(2)}) collective-permute-start(f32[75,4,1]{2,1,0:T(4,128)} %get-tuple-element.1977), channel_id=1, source_target_pairs={{0,1},{1,2},{2,3},{3,4},{4,5},{5,6},{6,7},{7,8},{8,9},{9,10},{10,1... | collective-permute-start | bytes 3608 | tf_op jit(solution)/shard_map/ppermute | solution.py:17
  230.5 0.7 copy-start.4
  238.5 11.9 %collective-permute-start.22 = (f32[75,1,128]{2,1,0:T(1,128)S(1)}, f32[75,1,128]{2,1,0:T(1,128)S(1)}, u32[]{:S(2)}, u32[]{:S(2)}) collective-permute-start(f32[75,1,128]{2,1,0:T(1,128)S(1)} %get-tuple-element.1974), channel_id=1, source_target_pairs={{16,0},{32,16},{48,32},{64,48},{80,64},{96,80},{112,96},{17,1},{33... | collective-permute-start | bytes 115208 | tf_op jit(solution)/shard_map/ppermute | solution.py:20
  239.8 10.6 %collective-permute-start.23 = (f32[75,1,128]{2,1,0:T(1,128)S(1)}, f32[75,1,128]{2,1,0:T(1,128)S(1)}, u32[]{:S(2)}, u32[]{:S(2)}) collective-permute-start(f32[75,1,128]{2,1,0:T(1,128)S(1)} %get-tuple-element.1975), channel_id=1, source_target_pairs={{0,16},{16,32},{32,48},{48,64},{64,80},{80,96},{96,112},{1,17},{17... | collective-permute-start | bytes 115208 | tf_op jit(solution)/shard_map/ppermute | solution.py:17
  244.5 2.8 collective-permute-start.20
  244.5 5.9 %collective-permute-start.21 = (f32[75,4,1]{2,1,0:T(4,128)S(1)}, f32[75,4,1]{2,1,0:T(4,128)S(1)}, u32[]{:S(2)}, u32[]{:S(2)}) collective-permute-start(f32[75,4,1]{2,1,0:T(4,128)S(1)} %get-tuple-element.1971), channel_id=1, source_target_pairs={{0,1},{1,2},{2,3},{3,4},{4,5},{5,6},{6,7},{7,8},{8,9},{9,10},{10,1... | collective-permute-start | bytes 3608 | tf_op jit(solution)/shard_map/ppermute | solution.py:17
  254.6 22.1 %all-to-all-start.2 = ((f32[16,128,4]{0,2,1:T(4,128)}), f32[16,128,4]{0,2,1:T(4,128)S(1)}, u32[]{:S(2)}, u32[]{:S(2)}) async-start(f32[16,128,4]{0,2,1:T(4,128)} %bitcast.32), calls=%async_computation.2 | async-start | bytes 524288 | tf_op jit(solution)/shard_map/all_to_all | solution.py:72
  291.9 13.3 %collective-permute-start.26 = (f32[75,1,128]{2,1,0:T(1,128)}, f32[75,1,128]{2,1,0:T(1,128)}, u32[]{:S(2)}, u32[]{:S(2)}) collective-permute-start(f32[75,1,128]{2,1,0:T(1,128)} %get-tuple-element.1968), channel_id=1, source_target_pairs={{16,0},{32,16},{48,32},{64,48},{80,64},{96,80},{112,96},{17,1},{33... | collective-permute-start | bytes 115208 | tf_op jit(solution)/shard_map/ppermute | solution.py:20
  293.2 12.7 %collective-permute-start.27 = (f32[75,1,128]{2,1,0:T(1,128)}, f32[75,1,128]{2,1,0:T(1,128)}, u32[]{:S(2)}, u32[]{:S(2)}) collective-permute-start(f32[75,1,128]{2,1,0:T(1,128)} %get-tuple-element.1969), channel_id=1, source_target_pairs={{0,16},{16,32},{32,48},{48,64},{64,80},{80,96},{96,112},{1,17},{17... | collective-permute-start | bytes 115208 | tf_op jit(solution)/shard_map/ppermute | solution.py:17
  299.2 3.1 collective-permute-start.24
  299.2 6.1 %collective-permute-start.25 = (f32[75,4,1]{2,1,0:T(4,128)}, f32[75,4,1]{2,1,0:T(4,128)S(1)}, u32[]{:S(2)}, u32[]{:S(2)}) collective-permute-start(f32[75,4,1]{2,1,0:T(4,128)} %get-tuple-element.1965), channel_id=1, source_target_pairs={{0,1},{1,2},{2,3},{3,4},{4,5},{5,6},{6,7},{7,8},{8,9},{9,10},{10,1... | collective-permute-start | bytes 3608 | tf_op jit(solution)/shard_map/ppermute | solution.py:17
  305.3 0.7 copy-start.5
  313.2 11.9 %collective-permute-start.30 = (f32[75,1,128]{2,1,0:T(1,128)S(1)}, f32[75,1,128]{2,1,0:T(1,128)S(1)}, u32[]{:S(2)}, u32[]{:S(2)}) collective-permute-start(f32[75,1,128]{2,1,0:T(1,128)S(1)} %get-tuple-element.1962), channel_id=1, source_target_pairs={{16,0},{32,16},{48,32},{64,48},{80,64},{96,80},{112,96},{17,1},{33... | collective-permute-start | bytes 115208 | tf_op jit(solution)/shard_map/ppermute | solution.py:20
  314.5 10.6 %collective-permute-start.31 = (f32[75,1,128]{2,1,0:T(1,128)S(1)}, f32[75,1,128]{2,1,0:T(1,128)S(1)}, u32[]{:S(2)}, u32[]{:S(2)}) collective-permute-start(f32[75,1,128]{2,1,0:T(1,128)S(1)} %get-tuple-element.1963), channel_id=1, source_target_pairs={{0,16},{16,32},{32,48},{48,64},{64,80},{80,96},{96,112},{1,17},{17... | collective-permute-start | bytes 115208 | tf_op jit(solution)/shard_map/ppermute | solution.py:17
  319.2 2.8 collective-permute-start.28
  319.3 5.9 %collective-permute-start.29 = (f32[75,4,1]{2,1,0:T(4,128)S(1)}, f32[75,4,1]{2,1,0:T(4,128)S(1)}, u32[]{:S(2)}, u32[]{:S(2)}) collective-permute-start(f32[75,4,1]{2,1,0:T(4,128)S(1)} %get-tuple-element.1959), channel_id=1, source_target_pairs={{0,1},{1,2},{2,3},{3,4},{4,5},{5,6},{6,7},{7,8},{8,9},{9,10},{10,1... | collective-permute-start | bytes 3608 | tf_op jit(solution)/shard_map/ppermute | solution.py:17
  329.4 22.1 %all-to-all-start.3 = ((f32[16,128,4]{0,2,1:T(4,128)}), f32[16,128,4]{0,2,1:T(4,128)S(1)}, u32[]{:S(2)}, u32[]{:S(2)}) async-start(f32[16,128,4]{0,2,1:T(4,128)} %bitcast.42), calls=%async_computation.3 | async-start | bytes 524288 | tf_op jit(solution)/shard_map/all_to_all | solution.py:72
where the time goes:
time: 365 us; the launch traced here: 362 us
  starting transfers between devices  96.5 us (26%)
  waiting for transfers between devices  91.7 us (25%)
  other arithmetic  85.1 us (23%)
  blocking collectives  36.2 us (10%)
  loops' own time  21.6 us (6%)
  local copies, waits for them, and re-layouts  17.9 us (5%)
  matrix products  12.5 us (3%)
    dynamic_update_slice x1200, other arithmetic, column_solve(): lax.scan(sweep_down, start_pair, (centre, lower_band, upper_band, right))  74.6 us
    all_to_all x4, waiting for transfers between devices, couple(): lax.all_to_all(contribution.reshape(block_cells, peer_count, capacity), (...  57.7 us
    ppermute x16, starting transfers between devices, extended(): lax.ppermute(lax.slice_in_dim(block, block.shape[dim] - width, None, axis...  42.1 us
    all_to_all x4, starting transfers between devices, couple(): lax.all_to_all(contribution.reshape(block_cells, peer_count, capacity), (...  39 us
    psum x4, blocking collectives, couple(): summed = lax.psum(accumulated * air_factor, 'sec')  36.2 us
    ppermute x16, waiting for transfers between devices, extended(): lax.ppermute(lax.slice_in_dim(block, block.shape[dim] - width, None, axis...  19.7 us
    ppermute x16, starting transfers between devices, extended(): lax.ppermute(lax.slice_in_dim(block, 0, width, axis=dim), axis, backward)  15.4 us
    ppermute x16, waiting for transfers between devices, extended(): lax.ppermute(lax.slice_in_dim(block, 0, width, axis=dim), axis, backward)  14.3 us
  transfers between devices with their start and end apart: 36, of which 17 were waited for; matrix products, arithmetic and copies ran while one was open for 2% of the time, Pallas kernels for 0%

commit v1 on v0

--- a/solution.py
+++ b/solution.py
@@ -85,7 +85,8 @@
     accumulated = jnp.dot(
         arrived, one_hot, precision=lax.Precision.HIGHEST, preferred_element_type=jnp.float32
     )
-    summed = lax.psum(accumulated * air_factor, "sec")
+    payload = accumulated * air_factor
+    summed = jnp.sum(jax.lax.all_gather(payload, "sec"), 0)
     return summed.T.reshape(field_part.shape[1], field_part.shape[2])
 
 

time: 365 us -> 377 us (1.033)
  blocking collectives: 36.2 us -> 47.8 us
    all_gather x0 -> x4, blocking collectives: none -> 47.8 us  [couple(): summed = jnp.sum(jax.lax.all_gather(payload, 'sec'), 0)]
    psum x4 -> x0, blocking collectives: 36.2 us -> none  [couple(): summed = lax.psum(accumulated * air_factor, 'sec')]
where the time goes in v1:
time: 377 us; the launch traced here: 374 us
  starting transfers between devices  96.7 us (26%)
  waiting for transfers between devices  91.7 us (24%)
  other arithmetic  85.1 us (23%)
  blocking collectives  47.8 us (13%)
  loops' own time  21.6 us (6%)
  local copies, waits for them, and re-layouts  17.8 us (5%)
  matrix products  12.5 us (3%)
    dynamic_update_slice x1200, other arithmetic, column_solve(): lax.scan(sweep_down, start_pair, (centre, lower_band, upper_band, right))  74.6 us
    all_to_all x4, waiting for transfers between devices, couple(): lax.all_to_all(contribution.reshape(block_cells, peer_count, capacity), (...  57.7 us
    all_gather x4, blocking collectives, couple(): summed = jnp.sum(jax.lax.all_gather(payload, 'sec'), 0)  47.8 us
    ppermute x16, starting transfers between devices, extended(): lax.ppermute(lax.slice_in_dim(block, block.shape[dim] - width, None, axis...  42.4 us
    all_to_all x4, starting transfers between devices, couple(): lax.all_to_all(contribution.reshape(block_cells, peer_count, capacity), (...  39 us
    ppermute x16, waiting for transfers between devices, extended(): lax.ppermute(lax.slice_in_dim(block, block.shape[dim] - width, None, axis...  19.7 us
    ppermute x16, starting transfers between devices, extended(): lax.ppermute(lax.slice_in_dim(block, 0, width, axis=dim), axis, backward)  15.4 us
    ppermute x16, waiting for transfers between devices, extended(): lax.ppermute(lax.slice_in_dim(block, 0, width, axis=dim), axis, backward)  14.3 us
  transfers between devices with their start and end apart: 36, of which 17 were waited for; matrix products, arithmetic and copies ran while one was open for 2% of the time, Pallas kernels for 0%

profile of v1, /device:TPU:2, one launch (start us, length us, event | category | flops | bytes accessed | tf_op | source)
XLA Modules:
  0.0 374.3 jit_solution(11030811064749934293)
XLA Ops:
  1.1 52.6 %while.276 = (s32[]{:T(128)}, f32[4,128]{1,0:T(4,128)S(1)}, f32[4,128]{1,0:T(4,128)S(1)}, f32[75,4,128]{2,1,0:T(4,128)S(1)}, f32[75,4,128]{2,1,0:T(4,128)S(1)}, ...) while((s32[]{:T(128)}, f32[4,128]{1,0:T(4,128)S(1)}, ...), condition=%wide.region_1.2_spmd.clone, body=%wide.region_0.1_spmd.clone.sunk | while | flops 4611 | bytes 20603 | solution.py:40
  53.7 2.7 while.277
  57.6 2.9 collective-permute-start
  61.9 4.9 %collective-permute-start.3 = (f32[75,1,128]{2,1,0:T(1,128)S(1)}, f32[75,1,128]{2,1,0:T(1,128)S(1)}, u32[]{:S(2)}, u32[]{:S(2)}) collective-permute-start(f32[75,1,128]{2,1,0:T(1,128)S(1)} %get-tuple-element.2005), channel_id=1, source_target_pairs={{0,16},{16,32},{32,48},{48,64},{64,80},{80,96},{96,112},{1,17},{17... | collective-permute-start | bytes 115208 | tf_op jit(solution)/shard_map/ppermute | solution.py:17
  68.9 3.2 while.278
  72.1 2.7 while.279
  79.8 4.9 %collective-permute-start.7 = (f32[75,1,128]{2,1,0:T(1,128)}, f32[75,1,128]{2,1,0:T(1,128)S(1)}, u32[]{:S(2)}, u32[]{:S(2)}) collective-permute-start(f32[75,1,128]{2,1,0:T(1,128)} %get-tuple-element.1999), channel_id=1, source_target_pairs={{0,16},{16,32},{32,48},{48,64},{64,80},{80,96},{96,112},{1,17},{17... | collective-permute-start | bytes 115208 | tf_op jit(solution)/shard_map/ppermute | solution.py:17
  89.5 2.6 fusion.123
  92.1 16.9 %all-to-all-start = ((f32[16,128,4]{0,2,1:T(4,128)}), f32[16,128,4]{0,2,1:T(4,128)S(1)}, u32[]{:S(2)}, u32[]{:S(2)}) async-start(f32[16,128,4]{0,2,1:T(4,128)} %bitcast.13), calls=%async_computation | async-start | bytes 524288 | tf_op jit(solution)/shard_map/all_to_all | solution.py:72
  109.5 14.2 %all-to-all-done = f32[16,128,4]{0,2,1:T(4,128)S(1)} async-done(((f32[16,128,4]{0,2,1:T(4,128)}), f32[16,128,4]{0,2,1:T(4,128)S(1)}, u32[]{:S(2)}, u32[]{:S(2)}) %all-to-all-start) | async-done | bytes 32800 | tf_op jit(solution)/shard_map/all_to_all | solution.py:72
  124.3 12.0 %all-gather = f32[64,32]{1,0:T(8,128)S(1)} all-gather(f32[16,32]{1,0:T(8,128)S(1)} %convolution_multiply_fusion.3), channel_id=2, replica_groups=mesh['sec'=4,'lat'=8,'lon'=16] {'sec'}, dimensions={0}, use_global_device_ids=true | all-gather | bytes 10240 | tf_op jit(solution)/shard_map/all_gather | solution.py:89
  136.5 3.2 while.280
  139.7 2.7 while.281
  144.5 5.2 %collective-permute-start.11 = (f32[75,1,128]{2,1,0:T(1,128)}, f32[75,1,128]{2,1,0:T(1,128)}, u32[]{:S(2)}, u32[]{:S(2)}) collective-permute-start(f32[75,1,128]{2,1,0:T(1,128)} %get-tuple-element.1993), channel_id=1, source_target_pairs={{0,16},{16,32},{32,48},{48,64},{64,80},{80,96},{96,112},{1,17},{17... | collective-permute-start | bytes 115208 | tf_op jit(solution)/shard_map/ppermute | solution.py:17
  153.6 3.0 collective-permute-done.9
  158.6 3.0 while.282
  161.7 2.7 while.283
  165.8 4.7 %collective-permute-start.15 = (f32[75,1,128]{2,1,0:T(1,128)S(1)}, f32[75,1,128]{2,1,0:T(1,128)S(1)}, u32[]{:S(2)}, u32[]{:S(2)}) collective-permute-start(f32[75,1,128]{2,1,0:T(1,128)S(1)} %get-tuple-element.1987), channel_id=1, source_target_pairs={{0,16},{16,32},{32,48},{48,64},{64,80},{80,96},{96,112},{1,17},{17... | collective-permute-start | bytes 115208 | tf_op jit(solution)/shard_map/ppermute | solution.py:17
  173.5 3.1 collective-permute-done.13
  178.3 2.6 fusion.124
  180.9 7.4 %all-to-all-start.1 = ((f32[16,128,4]{0,2,1:T(4,128)}), f32[16,128,4]{0,2,1:T(4,128)S(1)}, u32[]{:S(2)}, u32[]{:S(2)}) async-start(f32[16,128,4]{0,2,1:T(4,128)} %bitcast.24), calls=%async_computation.1 | async-start | bytes 524288 | tf_op jit(solution)/shard_map/all_to_all | solution.py:72
  188.3 14.7 %all-to-all-done.1 = f32[16,128,4]{0,2,1:T(4,128)S(1)} async-done(((f32[16,128,4]{0,2,1:T(4,128)}), f32[16,128,4]{0,2,1:T(4,128)S(1)}, u32[]{:S(2)}, u32[]{:S(2)}) %all-to-all-start.1) | async-done | bytes 32800 | tf_op jit(solution)/shard_map/all_to_all | solution.py:72
  203.5 11.9 %all-gather.1 = f32[64,32]{1,0:T(8,128)S(1)} all-gather(f32[16,32]{1,0:T(8,128)S(1)} %convolution_multiply_fusion.2), channel_id=3, replica_groups=mesh['sec'=4,'lat'=8,'lon'=16] {'sec'}, dimensions={0}, use_global_device_ids=true | all-gather | bytes 10240 | tf_op jit(solution)/shard_map/all_gather | solution.py:89
  215.7 3.2 while.284
  218.9 2.7 while.285
  223.7 5.2 %collective-permute-start.19 = (f32[75,1,128]{2,1,0:T(1,128)}, f32[75,1,128]{2,1,0:T(1,128)}, u32[]{:S(2)}, u32[]{:S(2)}) collective-permute-start(f32[75,1,128]{2,1,0:T(1,128)} %get-tuple-element.1981), channel_id=1, source_target_pairs={{0,16},{16,32},{32,48},{48,64},{64,80},{80,96},{96,112},{1,17},{17... | collective-permute-start | bytes 115208 | tf_op jit(solution)/shard_map/ppermute | solution.py:17
  230.2 2.5 collective-permute-done.16
  232.7 3.0 collective-permute-done.17
  237.7 3.0 while.286
  240.8 2.7 while.287
  245.0 4.5 %collective-permute-start.23 = (f32[75,1,128]{2,1,0:T(1,128)S(1)}, f32[75,1,128]{2,1,0:T(1,128)S(1)}, u32[]{:S(2)}, u32[]{:S(2)}) collective-permute-start(f32[75,1,128]{2,1,0:T(1,128)S(1)} %get-tuple-element.1975), channel_id=1, source_target_pairs={{0,16},{16,32},{32,48},{48,64},{64,80},{80,96},{96,112},{1,17},{17... | collective-permute-start | bytes 115208 | tf_op jit(solution)/shard_map/ppermute | solution.py:17
  252.5 3.1 collective-permute-done.21
  257.2 2.6 fusion.125
  259.8 7.4 %all-to-all-start.2 = ((f32[16,128,4]{0,2,1:T(4,128)}), f32[16,128,4]{0,2,1:T(4,128)S(1)}, u32[]{:S(2)}, u32[]{:S(2)}) async-start(f32[16,128,4]{0,2,1:T(4,128)} %bitcast.34), calls=%async_computation.2 | async-start | bytes 524288 | tf_op jit(solution)/shard_map/all_to_all | solution.py:72
  267.2 14.7 %all-to-all-done.2 = f32[16,128,4]{0,2,1:T(4,128)S(1)} async-done(((f32[16,128,4]{0,2,1:T(4,128)}), f32[16,128,4]{0,2,1:T(4,128)S(1)}, u32[]{:S(2)}, u32[]{:S(2)}) %all-to-all-start.2) | async-done | bytes 32800 | tf_op jit(solution)/shard_map/all_to_all | solution.py:72
  282.4 11.9 %all-gather.2 = f32[64,32]{1,0:T(8,128)S(1)} all-gather(f32[16,32]{1,0:T(8,128)S(1)} %convolution_multiply_fusion.1), channel_id=4, replica_groups=mesh['sec'=4,'lat'=8,'lon'=16] {'sec'}, dimensions={0}, use_global_device_ids=true | all-gather | bytes 10240 | tf_op jit(solution)/shard_map/all_gather | solution.py:89
  294.6 3.2 while.288
  297.8 2.7 while.289
  302.6 5.4 %collective-permute-start.27 = (f32[75,1,128]{2,1,0:T(1,128)}, f32[75,1,128]{2,1,0:T(1,128)}, u32[]{:S(2)}, u32[]{:S(2)}) collective-permute-start(f32[75,1,128]{2,1,0:T(1,128)} %get-tuple-element.1969), channel_id=1, source_target_pairs={{0,16},{16,32},{32,48},{48,64},{64,80},{80,96},{96,112},{1,17},{17... | collective-permute-start | bytes 115208 | tf_op jit(solution)/shard_map/ppermute | solution.py:17
  311.9 3.0 collective-permute-done.25
  316.9 3.0 while.290
  320.0 2.7 while.291
  324.2 4.5 %collective-permute-start.31 = (f32[75,1,128]{2,1,0:T(1,128)S(1)}, f32[75,1,128]{2,1,0:T(1,128)S(1)}, u32[]{:S(2)}, u32[]{:S(2)}) collective-permute-start(f32[75,1,128]{2,1,0:T(1,128)S(1)} %get-tuple-element.1963), channel_id=1, source_target_pairs={{0,16},{16,32},{32,48},{48,64},{64,80},{80,96},{96,112},{1,17},{17... | collective-permute-start | bytes 115208 | tf_op jit(solution)/shard_map/ppermute | solution.py:17
  331.6 3.1 collective-permute-done.29
  336.4 2.6 fusion.126
  339.0 7.4 %all-to-all-start.3 = ((f32[16,128,4]{0,2,1:T(4,128)}), f32[16,128,4]{0,2,1:T(4,128)S(1)}, u32[]{:S(2)}, u32[]{:S(2)}) async-start(f32[16,128,4]{0,2,1:T(4,128)} %bitcast.45), calls=%async_computation.3 | async-start | bytes 524288 | tf_op jit(solution)/shard_map/all_to_all | solution.py:72
  347.0 14.0 %all-to-all-done.3 = f32[16,128,4]{0,2,1:T(4,128)S(1)} async-done(((f32[16,128,4]{0,2,1:T(4,128)}), f32[16,128,4]{0,2,1:T(4,128)S(1)}, u32[]{:S(2)}, u32[]{:S(2)}) %all-to-all-start.3) | async-done | bytes 32800 | tf_op jit(solution)/shard_map/all_to_all | solution.py:72
  361.6 11.9 %all-gather.3 = f32[64,32]{1,0:T(8,128)S(1)} all-gather(f32[16,32]{1,0:T(8,128)S(1)} %convolution_multiply_fusion), channel_id=5, replica_groups=mesh['sec'=4,'lat'=8,'lon'=16] {'sec'}, dimensions={0}, use_global_device_ids=true | all-gather | bytes 10240 | tf_op jit(solution)/shard_map/all_gather | solution.py:89
  (1402 shorter events, 133.5 us)
Async XLA Ops:
  0.0 66.8 %copy-start.9 = (s32[1,1,1,128,4]{3,4,2,1,0:T(4,128)S(1)}, s32[1,1,1,128,4]{3,4,2,1,0:T(4,128)}, u32[]{:S(2)}) copy-start(s32[1,1,1,128,4]{3,4,2,1,0:T(4,128)} %param.57) | copy-start | bytes 6148
  0.0 67.1 %copy-start.6 = (s32[4,128]{1,0:T(4,128)S(1)}, s32[4,128]{1,0:T(4,128)}, u32[]{:S(2)}) copy-start(s32[4,128]{1,0:T(4,128)} %param.55) | copy-start | bytes 6148
  1.1 73.8 %copy-start = (bf16[1,75,4,128]{3,2,1,0:T(4,128)(2,1)S(1)}, bf16[1,75,4,128]{3,2,1,0:T(4,128)(2,1)}, u32[]{:S(2)}) copy-start(bf16[1,75,4,128]{3,2,1,0:T(4,128)(2,1)} %param.53) | copy-start | bytes 230404
  1.1 73.8 %copy-start.1 = (bf16[1,75,4,128]{3,2,1,0:T(4,128)(2,1)S(1)}, bf16[1,75,4,128]{3,2,1,0:T(4,128)(2,1)}, u32[]{:S(2)}) copy-start(bf16[1,75,4,128]{3,2,1,0:T(4,128)(2,1)} %param.54) | copy-start | bytes 230404
  57.4 27.3 %copy-start.2 = (bf16[1,1,1,16,16,512]{5,4,3,2,1,0:T(8,128)(2,1)S(1)}, bf16[1,1,1,16,16,512]{5,4,3,2,1,0:T(8,128)(2,1)}, u32[]{:S(2)}) copy-start(bf16[1,1,1,16,16,512]{5,4,3,2,1,0:T(8,128)(2,1)} %param.56) | copy-start | bytes 786436
  57.6 9.5 %collective-permute-start = (f32[75,4,1]{2,1,0:T(4,128)S(1)}, f32[75,4,1]{2,1,0:T(4,128)S(1)}, u32[]{:S(2)}, u32[]{:S(2)}) collective-permute-start(f32[75,4,1]{2,1,0:T(4,128)S(1)} %get-tuple-element.2000), channel_id=1, source_target_pairs={{1,0},{2,1},{3,2},{4,3},{5,4},{6,5},{7,6},{8,7},{9,8},{10,9},{11,1... | collective-permute-start | bytes 3608 | tf_op jit(solution)/shard_map/ppermute | solution.py:20
  60.5 6.6 %collective-permute-start.1 = (f32[75,4,1]{2,1,0:T(4,128)S(1)}, f32[75,4,1]{2,1,0:T(4,128)S(1)}, u32[]{:S(2)}, u32[]{:S(2)}) collective-permute-start(f32[75,4,1]{2,1,0:T(4,128)S(1)} %get-tuple-element.2001), channel_id=1, source_target_pairs={{0,1},{1,2},{2,3},{3,4},{4,5},{5,6},{6,7},{7,8},{8,9},{9,10},{10,1... | collective-permute-start | bytes 3608 | tf_op jit(solution)/shard_map/ppermute | solution.py:17
  60.6 6.6 %collective-permute-start.2 = (f32[75,1,128]{2,1,0:T(1,128)S(1)}, f32[75,1,128]{2,1,0:T(1,128)S(1)}, u32[]{:S(2)}, u32[]{:S(2)}) collective-permute-start(f32[75,1,128]{2,1,0:T(1,128)S(1)} %get-tuple-element.2004), channel_id=1, source_target_pairs={{16,0},{32,16},{48,32},{64,48},{80,64},{96,80},{112,96},{17,1},{33... | collective-permute-start | bytes 115208 | tf_op jit(solution)/shard_map/ppermute | solution.py:20
  61.9 6.5 %collective-permute-start.3 = (f32[75,1,128]{2,1,0:T(1,128)S(1)}, f32[75,1,128]{2,1,0:T(1,128)S(1)}, u32[]{:S(2)}, u32[]{:S(2)}) collective-permute-start(f32[75,1,128]{2,1,0:T(1,128)S(1)} %get-tuple-element.2005), channel_id=1, source_target_pairs={{0,16},{16,32},{32,48},{48,64},{64,80},{80,96},{96,112},{1,17},{17... | collective-permute-start | bytes 115208 | tf_op jit(solution)/shard_map/ppermute | solution.py:17
  67.1 22.3 %copy-start.7 = (pred[512]{0:T(512)(128)(4,1)}, pred[512]{0:T(512)(128)(4,1)S(1)}, u32[]{:S(2)}) copy-start(pred[512]{0:T(512)(128)(4,1)S(1)} %compare_and_fusion) | copy-start | bytes 1540
  75.8 11.1 %collective-permute-start.4 = (f32[75,4,1]{2,1,0:T(4,128)}, f32[75,4,1]{2,1,0:T(4,128)}, u32[]{:S(2)}, u32[]{:S(2)}) collective-permute-start(f32[75,4,1]{2,1,0:T(4,128)} %get-tuple-element.1994), channel_id=1, source_target_pairs={{1,0},{2,1},{3,2},{4,3},{5,4},{6,5},{7,6},{8,7},{9,8},{10,9},{11,1... | collective-permute-start | bytes 3608 | tf_op jit(solution)/shard_map/ppermute | solution.py:20
  77.9 9.0 %collective-permute-start.5 = (f32[75,4,1]{2,1,0:T(4,128)}, f32[75,4,1]{2,1,0:T(4,128)}, u32[]{:S(2)}, u32[]{:S(2)}) collective-permute-start(f32[75,4,1]{2,1,0:T(4,128)} %get-tuple-element.1995), channel_id=1, source_target_pairs={{0,1},{1,2},{2,3},{3,4},{4,5},{5,6},{6,7},{7,8},{8,9},{9,10},{10,1... | collective-permute-start | bytes 3608 | tf_op jit(solution)/shard_map/ppermute | solution.py:17
  78.6 8.3 %collective-permute-start.6 = (f32[75,1,128]{2,1,0:T(1,128)}, f32[75,1,128]{2,1,0:T(1,128)S(1)}, u32[]{:S(2)}, u32[]{:S(2)}) collective-permute-start(f32[75,1,128]{2,1,0:T(1,128)} %get-tuple-element.1998), channel_id=1, source_target_pairs={{16,0},{32,16},{48,32},{64,48},{80,64},{96,80},{112,96},{17,1},{33... | collective-permute-start | bytes 115208 | tf_op jit(solution)/shard_map/ppermute | solution.py:20
  79.8 7.0 %collective-permute-start.7 = (f32[75,1,128]{2,1,0:T(1,128)}, f32[75,1,128]{2,1,0:T(1,128)S(1)}, u32[]{:S(2)}, u32[]{:S(2)}) collective-permute-start(f32[75,1,128]{2,1,0:T(1,128)} %get-tuple-element.1999), channel_id=1, source_target_pairs={{0,16},{16,32},{32,48},{48,64},{64,80},{80,96},{96,112},{1,17},{17... | collective-permute-start | bytes 115208 | tf_op jit(solution)/shard_map/ppermute | solution.py:17
  89.4 19.7 %copy-start.11 = (s32[1,1,1,128]{3,2,1,0:T(1,128)S(1)}, s32[1,1,1,128]{3,2,1,0:T(1,128)}, u32[]{:S(2)}) copy-start(s32[1,1,1,128]{3,2,1,0:T(1,128)} %param.59) | copy-start | bytes 1540
  89.4 19.8 %copy-start.10 = (s32[1,1,1,128,4]{3,4,2,1,0:T(4,128)S(1)}, s32[1,1,1,128,4]{3,4,2,1,0:T(4,128)}, u32[]{:S(2)}) copy-start(s32[1,1,1,128,4]{3,4,2,1,0:T(4,128)} %param.58) | copy-start | bytes 6148
  92.1 31.6 %all-to-all-start = ((f32[16,128,4]{0,2,1:T(4,128)}), f32[16,128,4]{0,2,1:T(4,128)S(1)}, u32[]{:S(2)}, u32[]{:S(2)}) async-start(f32[16,128,4]{0,2,1:T(4,128)} %bitcast.13), calls=%async_computation | async-start | bytes 524288 | tf_op jit(solution)/shard_map/all_to_all | solution.py:72
  143.2 13.3 %collective-permute-start.10 = (f32[75,1,128]{2,1,0:T(1,128)}, f32[75,1,128]{2,1,0:T(1,128)}, u32[]{:S(2)}, u32[]{:S(2)}) collective-permute-start(f32[75,1,128]{2,1,0:T(1,128)} %get-tuple-element.1992), channel_id=1, source_target_pairs={{16,0},{32,16},{48,32},{64,48},{80,64},{96,80},{112,96},{17,1},{33... | collective-permute-start | bytes 115208 | tf_op jit(solution)/shard_map/ppermute | solution.py:20
  144.5 12.7 %collective-permute-start.11 = (f32[75,1,128]{2,1,0:T(1,128)}, f32[75,1,128]{2,1,0:T(1,128)}, u32[]{:S(2)}, u32[]{:S(2)}) collective-permute-start(f32[75,1,128]{2,1,0:T(1,128)} %get-tuple-element.1993), channel_id=1, source_target_pairs={{0,16},{16,32},{32,48},{48,64},{64,80},{80,96},{96,112},{1,17},{17... | collective-permute-start | bytes 115208 | tf_op jit(solution)/shard_map/ppermute | solution.py:17
  150.5 3.1 collective-permute-start.8
  150.5 6.1 %collective-permute-start.9 = (f32[75,4,1]{2,1,0:T(4,128)}, f32[75,4,1]{2,1,0:T(4,128)S(1)}, u32[]{:S(2)}, u32[]{:S(2)}) collective-permute-start(f32[75,4,1]{2,1,0:T(4,128)} %get-tuple-element.1989), channel_id=1, source_target_pairs={{0,1},{1,2},{2,3},{3,4},{4,5},{5,6},{6,7},{7,8},{8,9},{9,10},{10,1... | collective-permute-start | bytes 3608 | tf_op jit(solution)/shard_map/ppermute | solution.py:17
  156.6 0.7 copy-start.3
  164.5 13.7 %copy-start.8 = (pred[512]{0:T(512)(128)(4,1)S(1)}, pred[512]{0:T(512)(128)(4,1)}, u32[]{:S(2)}) copy-start(pred[512]{0:T(512)(128)(4,1)} %copy-done.7) | copy-start | bytes 1540
  164.5 12.1 %collective-permute-start.14 = (f32[75,1,128]{2,1,0:T(1,128)S(1)}, f32[75,1,128]{2,1,0:T(1,128)S(1)}, u32[]{:S(2)}, u32[]{:S(2)}) collective-permute-start(f32[75,1,128]{2,1,0:T(1,128)S(1)} %get-tuple-element.1986), channel_id=1, source_target_pairs={{16,0},{32,16},{48,32},{64,48},{80,64},{96,80},{112,96},{17,1},{33... | collective-permute-start | bytes 115208 | tf_op jit(solution)/shard_map/ppermute | solution.py:20
  165.8 10.8 %collective-permute-start.15 = (f32[75,1,128]{2,1,0:T(1,128)S(1)}, f32[75,1,128]{2,1,0:T(1,128)S(1)}, u32[]{:S(2)}, u32[]{:S(2)}) collective-permute-start(f32[75,1,128]{2,1,0:T(1,128)S(1)} %get-tuple-element.1987), channel_id=1, source_target_pairs={{0,16},{16,32},{32,48},{48,64},{64,80},{80,96},{96,112},{1,17},{17... | collective-permute-start | bytes 115208 | tf_op jit(solution)/shard_map/ppermute | solution.py:17
  170.7 2.8 collective-permute-start.12
  170.8 5.9 %collective-permute-start.13 = (f32[75,4,1]{2,1,0:T(4,128)S(1)}, f32[75,4,1]{2,1,0:T(4,128)S(1)}, u32[]{:S(2)}, u32[]{:S(2)}) collective-permute-start(f32[75,4,1]{2,1,0:T(4,128)S(1)} %get-tuple-element.1983), channel_id=1, source_target_pairs={{0,1},{1,2},{2,3},{3,4},{4,5},{5,6},{6,7},{7,8},{8,9},{9,10},{10,1... | collective-permute-start | bytes 3608 | tf_op jit(solution)/shard_map/ppermute | solution.py:17
  180.9 22.1 %all-to-all-start.1 = ((f32[16,128,4]{0,2,1:T(4,128)}), f32[16,128,4]{0,2,1:T(4,128)S(1)}, u32[]{:S(2)}, u32[]{:S(2)}) async-start(f32[16,128,4]{0,2,1:T(4,128)} %bitcast.24), calls=%async_computation.1 | async-start | bytes 524288 | tf_op jit(solution)/shard_map/all_to_all | solution.py:72
  222.4 13.3 %collective-permute-start.18 = (f32[75,1,128]{2,1,0:T(1,128)}, f32[75,1,128]{2,1,0:T(1,128)}, u32[]{:S(2)}, u32[]{:S(2)}) collective-permute-start(f32[75,1,128]{2,1,0:T(1,128)} %get-tuple-element.1980), channel_id=1, source_target_pairs={{16,0},{32,16},{48,32},{64,48},{80,64},{96,80},{112,96},{17,1},{33... | collective-permute-start | bytes 115208 | tf_op jit(solution)/shard_map/ppermute | solution.py:20
  223.7 12.7 %collective-permute-start.19 = (f32[75,1,128]{2,1,0:T(1,128)}, f32[75,1,128]{2,1,0:T(1,128)}, u32[]{:S(2)}, u32[]{:S(2)}) collective-permute-start(f32[75,1,128]{2,1,0:T(1,128)} %get-tuple-element.1981), channel_id=1, source_target_pairs={{0,16},{16,32},{32,48},{48,64},{64,80},{80,96},{96,112},{1,17},{17... | collective-permute-start | bytes 115208 | tf_op jit(solution)/shard_map/ppermute | solution.py:17
  229.7 3.1 collective-permute-start.16
  229.7 6.1 %collective-permute-start.17 = (f32[75,4,1]{2,1,0:T(4,128)}, f32[75,4,1]{2,1,0:T(4,128)S(1)}, u32[]{:S(2)}, u32[]{:S(2)}) collective-permute-start(f32[75,4,1]{2,1,0:T(4,128)} %get-tuple-element.1977), channel_id=1, source_target_pairs={{0,1},{1,2},{2,3},{3,4},{4,5},{5,6},{6,7},{7,8},{8,9},{9,10},{10,1... | collective-permute-start | bytes 3608 | tf_op jit(solution)/shard_map/ppermute | solution.py:17
  235.7 0.7 copy-start.4
  243.7 11.9 %collective-permute-start.22 = (f32[75,1,128]{2,1,0:T(1,128)S(1)}, f32[75,1,128]{2,1,0:T(1,128)S(1)}, u32[]{:S(2)}, u32[]{:S(2)}) collective-permute-start(f32[75,1,128]{2,1,0:T(1,128)S(1)} %get-tuple-element.1974), channel_id=1, source_target_pairs={{16,0},{32,16},{48,32},{64,48},{80,64},{96,80},{112,96},{17,1},{33... | collective-permute-start | bytes 115208 | tf_op jit(solution)/shard_map/ppermute | solution.py:20
  245.0 10.6 %collective-permute-start.23 = (f32[75,1,128]{2,1,0:T(1,128)S(1)}, f32[75,1,128]{2,1,0:T(1,128)S(1)}, u32[]{:S(2)}, u32[]{:S(2)}) collective-permute-start(f32[75,1,128]{2,1,0:T(1,128)S(1)} %get-tuple-element.1975), channel_id=1, source_target_pairs={{0,16},{16,32},{32,48},{48,64},{64,80},{80,96},{96,112},{1,17},{17... | collective-permute-start | bytes 115208 | tf_op jit(solution)/shard_map/ppermute | solution.py:17
  249.7 2.8 collective-permute-start.20
  249.7 5.9 %collective-permute-start.21 = (f32[75,4,1]{2,1,0:T(4,128)S(1)}, f32[75,4,1]{2,1,0:T(4,128)S(1)}, u32[]{:S(2)}, u32[]{:S(2)}) collective-permute-start(f32[75,4,1]{2,1,0:T(4,128)S(1)} %get-tuple-element.1971), channel_id=1, source_target_pairs={{0,1},{1,2},{2,3},{3,4},{4,5},{5,6},{6,7},{7,8},{8,9},{9,10},{10,1... | collective-permute-start | bytes 3608 | tf_op jit(solution)/shard_map/ppermute | solution.py:17
  259.8 22.1 %all-to-all-start.2 = ((f32[16,128,4]{0,2,1:T(4,128)}), f32[16,128,4]{0,2,1:T(4,128)S(1)}, u32[]{:S(2)}, u32[]{:S(2)}) async-start(f32[16,128,4]{0,2,1:T(4,128)} %bitcast.34), calls=%async_computation.2 | async-start | bytes 524288 | tf_op jit(solution)/shard_map/all_to_all | solution.py:72
  301.4 13.5 %collective-permute-start.26 = (f32[75,1,128]{2,1,0:T(1,128)}, f32[75,1,128]{2,1,0:T(1,128)}, u32[]{:S(2)}, u32[]{:S(2)}) collective-permute-start(f32[75,1,128]{2,1,0:T(1,128)} %get-tuple-element.1968), channel_id=1, source_target_pairs={{16,0},{32,16},{48,32},{64,48},{80,64},{96,80},{112,96},{17,1},{33... | collective-permute-start | bytes 115208 | tf_op jit(solution)/shard_map/ppermute | solution.py:20
  302.6 12.9 %collective-permute-start.27 = (f32[75,1,128]{2,1,0:T(1,128)}, f32[75,1,128]{2,1,0:T(1,128)}, u32[]{:S(2)}, u32[]{:S(2)}) collective-permute-start(f32[75,1,128]{2,1,0:T(1,128)} %get-tuple-element.1969), channel_id=1, source_target_pairs={{0,16},{16,32},{32,48},{48,64},{64,80},{80,96},{96,112},{1,17},{17... | collective-permute-start | bytes 115208 | tf_op jit(solution)/shard_map/ppermute | solution.py:17
  308.8 3.1 collective-permute-start.24
  308.8 6.1 %collective-permute-start.25 = (f32[75,4,1]{2,1,0:T(4,128)}, f32[75,4,1]{2,1,0:T(4,128)S(1)}, u32[]{:S(2)}, u32[]{:S(2)}) collective-permute-start(f32[75,4,1]{2,1,0:T(4,128)} %get-tuple-element.1965), channel_id=1, source_target_pairs={{0,1},{1,2},{2,3},{3,4},{4,5},{5,6},{6,7},{7,8},{8,9},{9,10},{10,1... | collective-permute-start | bytes 3608 | tf_op jit(solution)/shard_map/ppermute | solution.py:17
  314.9 0.7 copy-start.5
  322.9 11.9 %collective-permute-start.30 = (f32[75,1,128]{2,1,0:T(1,128)S(1)}, f32[75,1,128]{2,1,0:T(1,128)S(1)}, u32[]{:S(2)}, u32[]{:S(2)}) collective-permute-start(f32[75,1,128]{2,1,0:T(1,128)S(1)} %get-tuple-element.1962), channel_id=1, source_target_pairs={{16,0},{32,16},{48,32},{64,48},{80,64},{96,80},{112,96},{17,1},{33... | collective-permute-start | bytes 115208 | tf_op jit(solution)/shard_map/ppermute | solution.py:20
  324.2 10.6 %collective-permute-start.31 = (f32[75,1,128]{2,1,0:T(1,128)S(1)}, f32[75,1,128]{2,1,0:T(1,128)S(1)}, u32[]{:S(2)}, u32[]{:S(2)}) collective-permute-start(f32[75,1,128]{2,1,0:T(1,128)S(1)} %get-tuple-element.1963), channel_id=1, source_target_pairs={{0,16},{16,32},{32,48},{48,64},{64,80},{80,96},{96,112},{1,17},{17... | collective-permute-start | bytes 115208 | tf_op jit(solution)/shard_map/ppermute | solution.py:17
  328.9 2.8 collective-permute-start.28
  328.9 5.9 %collective-permute-start.29 = (f32[75,4,1]{2,1,0:T(4,128)S(1)}, f32[75,4,1]{2,1,0:T(4,128)S(1)}, u32[]{:S(2)}, u32[]{:S(2)}) collective-permute-start(f32[75,4,1]{2,1,0:T(4,128)S(1)} %get-tuple-element.1959), channel_id=1, source_target_pairs={{0,1},{1,2},{2,3},{3,4},{4,5},{5,6},{6,7},{7,8},{8,9},{9,10},{10,1... | collective-permute-start | bytes 3608 | tf_op jit(solution)/shard_map/ppermute | solution.py:17
  339.0 22.1 %all-to-all-start.3 = ((f32[16,128,4]{0,2,1:T(4,128)}), f32[16,128,4]{0,2,1:T(4,128)S(1)}, u32[]{:S(2)}, u32[]{:S(2)}) async-start(f32[16,128,4]{0,2,1:T(4,128)} %bitcast.45), calls=%async_computation.3 | async-start | bytes 524288 | tf_op jit(solution)/shard_map/all_to_all | solution.py:72
